TPU v7x, 256 devices: a whole 4x4x8 slice. The times are simulated.
256 devices in a mesh: dp: 4 (over y), expert: 64 (over z, x, core).
Axes of the slice: x: 4, y: 4, z: 8, core: 2. Of those that a mesh axis runs over, the one named last changes fastest.
Arguments:
- hidden_states: bfloat16 [1024, 4, 4096], P('expert'), may hold values from -6 to 6
- routes: int32 [1024, 4, 8], P('expert'), may hold values from 0 to 63, all different within a row; in each aligned block of 64 rows (0 to 63, 64 to 127, ..., all dimensions but the last counted through in order) at most 16 rows name the same one
- route_weight: float32 [1024, 4, 8], P('expert'), may hold values from 0.05 to 1
- finish_step: int32 [1024], P('expert'), may hold values from 1 to 4
- group_keep: int32 [64], P('expert'), may hold values from 0 to 1
- dest_slot: int32 [1024], P('expert'), may hold values from 0 to 1023, as said below
- w_gate: bfloat16 [64, 4096, 1536], P('expert', None, 'dp'), may hold values from -0.09375 to 0.09375
- w_up: bfloat16 [64, 4096, 1536], P('expert', None, 'dp'), may hold values from -0.09375 to 0.09375
- w_down: bfloat16 [64, 1536, 4096], P('expert', 'dp'), may hold values from -0.15625 to 0.15625
Outputs:
- trainer_rows: bfloat16 [1024, 4, 4096], P(('dp', 'expert'))
Inputs may be any that keep to these rules, and one draw needn't show every extreme that they name: `routes`: in the 64 row-steps of one prompt group (rows g * 16 to (g + 1) * 16 - 1, all steps), no expert is named more than 16 times, a bound that some block reaches; a row names 8 different experts at each step. dest_slot is a permutation of the slots; row r of group g = r // 16 goes to a slot (d * 64 + g) * 4 + i with 0 <= d < 4 and 0 <= i < 4.
All inputs are finite; a program needn't handle non-finite values.
Results may differ from a plain program's by a relative error of at most 0.0049.
Values may be sent and summed in bfloat16 or wider, within the bound.
No kernel may reach another device: no remote copies, remote signals or barrier semaphores. Data moves between devices by JAX's collectives and lax.ppermute only.
A program may use at most 128 MiB of HBM per device.

v0:
```python
import jax
import jax.numpy as jnp
from jax import lax
from jax.sharding import PartitionSpec as P

MOST_BASE = 16


def exchange_gather(matrix, replica, replica_count):
    width = matrix.shape[1] // replica_count
    pieces = [lax.dynamic_slice_in_dim(matrix, replica * width, width, axis=1)]
    for shift in range(1, replica_count):
        start = (replica + shift) % replica_count * width
        outgoing = lax.dynamic_slice_in_dim(matrix, start, width, axis=1)
        pairs = [(i, (i + shift) % replica_count) for i in range(replica_count)]
        pieces.append(lax.ppermute(outgoing, "dp", pairs))
    return pieces


def exchange_all(block, replica_count):
    pieces = [block]
    for shift in range(1, replica_count):
        pairs = [(i, (i + shift) % replica_count) for i in range(replica_count)]
        pieces.append(lax.ppermute(block, "dp", pairs))
    return jnp.stack(pieces, axis=0)


def body(
    hidden_states, routes, route_weight, finish_step, group_keep, dest_slot, w_gate, w_up, w_down
):
    expert_count = lax.axis_size("expert")
    replica_count = lax.axis_size("dp")
    replica = lax.axis_index("dp")
    row_count, step_count, model_width = hidden_states.shape
    top_count = routes.shape[2]
    hidden_part = w_down.shape[1]
    columns = model_width // replica_count
    tokens = row_count * step_count
    slot_count = min(tokens, max(MOST_BASE, 2 * tokens * top_count // expert_count))
    slot_count = -(-slot_count // replica_count) * replica_count
    part = slot_count // replica_count
    down_cols = exchange_gather(w_down[0], replica, replica_count)
    step_ids = lax.broadcasted_iota(jnp.int32, (row_count, step_count), 1)
    live_mask = ((step_ids < finish_step[:, None]) & (group_keep[0] == 1)).reshape(tokens)
    gate_share = route_weight / jnp.sum(route_weight, axis=2, keepdims=True)
    expert_ids = lax.broadcasted_iota(jnp.int32, (1, 1, expert_count), 2)
    picked = (routes.reshape(tokens, top_count, 1) == expert_ids) & live_mask[:, None, None]
    hit_mask = jnp.sum(picked.astype(jnp.int32), axis=1)
    share_wide = jnp.broadcast_to(gate_share.reshape(tokens, top_count, 1), picked.shape)
    weight = jnp.sum(jnp.where(picked, share_wide, jnp.zeros_like(share_wide)), axis=1)
    prior_hits = jnp.cumsum(hit_mask, axis=0) - hit_mask
    flat_inputs = hidden_states.reshape(tokens, model_width)
    chunks = 2 if part % 2 == 0 else 1
    sub = part // chunks
    member_ids = lax.broadcasted_iota(jnp.int32, (1, 1, replica_count, 1), 2)
    within_ids = lax.broadcasted_iota(jnp.int32, (1, 1, 1, sub), 3)
    combined = jnp.zeros((tokens, columns), jnp.float32)
    outgoings = []
    for chunk in range(chunks):
        slot_ids = replica * part + chunk * sub + lax.broadcasted_iota(jnp.int32, (1, 1, sub), 2)
        placement = (hit_mask[:, :, None] == 1) & (prior_hits[:, :, None] == slot_ids)
        placement = placement.reshape(tokens, expert_count * sub)
        outgoings.append(
            lax.dot_general(
                placement.astype(jnp.bfloat16),
                flat_inputs,
                (((0,), (0,)), ((), ())),
                preferred_element_type=jnp.float32,
            ).astype(jnp.bfloat16)
        )
    if chunks > 1:
        down_cols, outgoings[1] = lax.optimization_barrier((down_cols, outgoings[1]))
    down_stack = jnp.stack(down_cols, axis=0)
    for chunk in range(chunks):
        outgoing = outgoings[chunk]
        arrived = lax.all_to_all(outgoing, "expert", split_axis=0, concat_axis=0, tiled=True)
        gathered = lax.all_gather(arrived, "dp", axis=0, tiled=True)
        gate_part = jnp.dot(gathered, w_gate[0], preferred_element_type=jnp.float32)
        up_part = jnp.dot(gathered, w_up[0], preferred_element_type=jnp.float32)
        activated = (jax.nn.silu(gate_part) * up_part).astype(jnp.bfloat16)
        hidden_all = exchange_all(activated, replica_count)
        expert_cols = lax.dot_general(
            hidden_all, down_stack, (((0, 2), (0, 1)), ((), ())), preferred_element_type=jnp.float32
        ).astype(jnp.bfloat16)
        by_source = expert_cols.reshape(replica_count, expert_count, sub, columns).transpose(
            1, 0, 2, 3
        )
        returned_rows = lax.all_to_all(by_source, "expert", split_axis=0, concat_axis=0, tiled=True)
        all_slot_ids = member_ids * part + chunk * sub + within_ids
        weighted_place = jnp.where(
            (hit_mask[:, :, None, None] == 1) & (prior_hits[:, :, None, None] == all_slot_ids),
            weight[:, :, None, None],
            0.0,
        ).reshape(tokens, expert_count * replica_count * sub)
        combined = combined + jnp.dot(
            weighted_place,
            returned_rows.reshape(expert_count * replica_count * sub, columns).astype(jnp.float32),
            precision=lax.Precision.HIGH,
            preferred_element_type=jnp.float32,
        )
    share_rows = row_count // replica_count
    flat_device = dest_slot // share_rows
    target = flat_device // expert_count * share_rows + dest_slot % share_rows
    position_ids = lax.broadcasted_iota(jnp.int32, (replica_count * share_rows, row_count), 0)
    arrangement = (target[None, :] == position_ids).astype(jnp.bfloat16)
    arranged = jnp.dot(
        arrangement,
        combined.astype(jnp.bfloat16).reshape(row_count, step_count * columns),
        preferred_element_type=jnp.float32,
    ).astype(jnp.bfloat16)
    arranged = arranged.reshape(replica_count, share_rows, step_count, columns)
    quarters = lax.all_to_all(arranged, "dp", split_axis=0, concat_axis=0, tiled=True)
    return quarters.transpose(1, 2, 0, 3).reshape(share_rows, step_count, model_width)


def solution(mesh):
    in_specs = (
        P("expert", None, None),
        P("expert", None, None),
        P("expert", None, None),
        P("expert"),
        P("expert"),
        P("expert"),
        P("expert", None, "dp"),
        P("expert", None, "dp"),
        P("expert", "dp", None),
    )
    out_specs = P(("dp", "expert"), None, None)
    return jax.shard_map(body, mesh=mesh, in_specs=in_specs, out_specs=out_specs, check_vma=False)
```

profile of v0, /device:TPU:2, one launch (start us, length us, event | category | flops | bytes accessed | tf_op | source)
XLA Modules:
  0.0 302.3 jit_solution(9261390843322471953)
XLA Ops:
  6.5 3.7 %dynamic-slice_bitcast_fusion = (bf16[384,1024]{1,0:T(8,128)(2,1)}, bf16[384,1024]{1,0:T(8,128)(2,1)}, bf16[384,1024]{1,0:T(8,128)(2,1)}, bf16[384,1024]{1,0:T(8,128)(2,1)}) fusion(bf16[1,384,4096]{2,1,0:T(8,128)(2,1)} %param.17, s32[]{:T(128)S(6)} %select_n.63, s32[]{:T(128)S(6)} %select_n.59, s32[]{:T(128)S(6)} %select_n.57, s32[]{:T(128)S(6)} %select_n.61), kind=kLoop, calls=%fused_computation.40 | loop fusion | bytes 6291472 | tf_op jit(solution)/shard_map/dynamic_slice | solution.py:14
  10.3 1.6 collective-permute-start.3
  11.9 2.9 collective-permute-start.4
  14.8 1.3 collective-permute-start.5
  17.0 0.2 convert_reduce_fusion
  17.8 2.0 reshape.213
  19.7 2.4 convolution_convert_fusion
  22.2 9.0 %collective-permute-done.3 = bf16[384,1024]{1,0:T(8,128)(2,1)} collective-permute-done((bf16[384,1024]{1,0:T(8,128)(2,1)}, bf16[384,1024]{1,0:T(8,128)(2,1)}, u32[]{:S(2)}, u32[]{:S(2)}) %collective-permute-start.3) | collective-permute-done | bytes 786464 | tf_op jit(solution)/shard_map/ppermute | solution.py:16
  31.2 18.0 %collective-permute-done.4 = bf16[384,1024]{1,0:T(8,128)(2,1)} collective-permute-done((bf16[384,1024]{1,0:T(8,128)(2,1)}, bf16[384,1024]{1,0:T(8,128)(2,1)}, u32[]{:S(2)}, u32[]{:S(2)}) %collective-permute-start.4) | collective-permute-done | bytes 786464 | tf_op jit(solution)/shard_map/ppermute | solution.py:16
  49.2 2.5 all_to_all.29
  51.7 40.9 %all_to_all.39 = bf16[64,2,4096]{2,1,0:T(2,128)(2,1)} all-to-all(bf16[64,2,4096]{2,1,0:T(2,128)(2,1)} %all_to_all.29), channel_id=1, replica_groups=mesh['dp'=4,'expert'=64] {'expert'}, dimensions={0} | all-to-all | bytes 2097152 | tf_op jit(solution)/shard_map/all_to_all | solution.py:76
  92.7 2.3 all_to_all.31
  95.1 2.4 convolution_convert_fusion.1
  97.5 2.5 all_to_all.25
  100.1 34.6 %all_to_all.40 = bf16[64,2,4096]{2,1,0:T(2,128)(2,1)} all-to-all(bf16[64,2,4096]{2,1,0:T(2,128)(2,1)} %all_to_all.25), channel_id=1, replica_groups=mesh['dp'=4,'expert'=64] {'expert'}, dimensions={0} | all-to-all | bytes 2097152 | tf_op jit(solution)/shard_map/all_to_all | solution.py:76
  134.6 2.3 all_to_all.27
  136.9 5.0 %all-gather.5.cloned.1.call-done = bf16[512,4096]{1,0:T(8,128)(2,1)} async-done(((bf16[128,4096]{1,0:T(8,128)(2,1)}), bf16[512,4096]{1,0:T(8,128)(2,1)}) %all-gather.5.cloned.1.call-update) | async-done | bytes 4194320 | tf_op jit(solution)/shard_map/all_gather | solution.py:77
  142.0 4.7 %fusion.4 = f32[512,384]{1,0:T(8,128)S(1)} fusion(bf16[512,4096]{1,0:T(8,128)(2,1)} %all-gather.5.cloned.1.call-done, bf16[1,4096,384]{2,1,0:T(8,128)(2,1)S(1)} %copy-done), kind=kOutput, calls=%fused_computation.8 | convolution fusion | flops 1610612736 | bytes 8126464 | tf_op jit(solution)/shard_map/dot_general | solution.py:78
  146.7 2.3 fusion.28
  149.0 1.2 collective-permute-start.8
  150.2 1.8 collective-permute-start.7
  152.0 0.6 collective-permute-start.6
  152.6 9.2 %collective-permute-done.8 = bf16[512,384]{1,0:T(8,128)(2,1)S(1)} collective-permute-done((bf16[512,384]{1,0:T(8,128)(2,1)S(1)}, bf16[512,384]{1,0:T(8,128)(2,1)S(1)}, u32[]{:S(2)}, u32[]{:S(2)}) %collective-permute-start.8) | collective-permute-done | bytes 393248 | tf_op jit(solution)/shard_map/ppermute | solution.py:24
  161.8 4.5 %collective-permute-done.7 = bf16[512,384]{1,0:T(8,128)(2,1)S(1)} collective-permute-done((bf16[512,384]{1,0:T(8,128)(2,1)S(1)}, bf16[512,384]{1,0:T(8,128)(2,1)S(1)}, u32[]{:S(2)}, u32[]{:S(2)}) %collective-permute-start.7) | collective-permute-done | bytes 393248 | tf_op jit(solution)/shard_map/ppermute | solution.py:24
  166.3 14.4 %collective-permute-done.6 = bf16[512,384]{1,0:T(8,128)(2,1)S(1)} collective-permute-done((bf16[512,384]{1,0:T(8,128)(2,1)S(1)}, bf16[512,384]{1,0:T(8,128)(2,1)S(1)}, u32[]{:S(2)}, u32[]{:S(2)}) %collective-permute-start.6) | collective-permute-done | bytes 393248 | tf_op jit(solution)/shard_map/ppermute | solution.py:24
  180.7 4.5 %bitcast_convert_fusion = bf16[512,1024]{1,0:T(8,128)(2,1)} fusion(bf16[1,512,384]{2,1,0:T(8,128)(2,1)S(1)} %bitcast.91, bf16[1,512,384]{2,1,0:T(8,128)(2,1)S(1)} %bitcast.93, bf16[1,512,384]{2,1,0:T(8,128)(2,1)S(1)} %bitcast.94, bf16[1,512,384]{2,1,0:T(8,128)(2,1)S(1)} %bitcast.88, bf16[1,384,1024]{2,1,0:T(8,128)(2,1)} %bitcast.16, ...), kind=kOutput, calls=%fused_computation.12 | convolution fusion | flops 1618214912 | bytes 5767168 | tf_op jit(solution)/shard_map/dot_general | solution.py:82
  185.2 2.2 reshape.215
  187.5 3.4 %copy.47 = bf16[4,64,2,1024]{3,2,0,1:T(2,128)(2,1)} copy(bf16[4,64,2,1024]{3,2,1,0:T(2,128)(2,1)} %reshape.215) | data formatting | bytes 2097152 | tf_op jit(solution)/shard_map/reshape | solution.py:85
  190.8 10.7 %all-to-all-start.3 = ((bf16[64,4,2,1024]{3,2,1,0:T(2,128)(2,1)}), bf16[64,4,2,1024]{3,2,1,0:T(2,128)(2,1)}, u32[]{:S(2)}, u32[]{:S(2)}) async-start(bf16[64,4,2,1024]{3,2,1,0:T(2,128)(2,1)} %bitcast.79), calls=%async_computation.3 | async-start | bytes 2097152 | tf_op jit(solution)/shard_map/all_to_all | solution.py:88
  201.6 3.2 %all-gather.3.cloned.1.call-done = bf16[512,4096]{1,0:T(8,128)(2,1)} async-done(((bf16[128,4096]{1,0:T(8,128)(2,1)}), bf16[512,4096]{1,0:T(8,128)(2,1)}) %all-gather.3.cloned.1.call-update) | async-done | bytes 4194320 | tf_op jit(solution)/shard_map/all_gather | solution.py:77
  204.8 4.7 %fusion.6 = f32[512,384]{1,0:T(8,128)S(1)} fusion(bf16[512,4096]{1,0:T(8,128)(2,1)} %all-gather.3.cloned.1.call-done, bf16[1,4096,384]{2,1,0:T(8,128)(2,1)S(1)} %copy-done), kind=kOutput, calls=%fused_computation.10 | convolution fusion | flops 1610612736 | bytes 8126464 | tf_op jit(solution)/shard_map/dot_general | solution.py:78
  209.5 2.3 fusion.31
  211.8 0.7 collective-permute-start.2
  212.5 1.8 collective-permute-start.1
  214.3 0.8 collective-permute-start
  215.1 8.8 %collective-permute-done.2 = bf16[512,384]{1,0:T(8,128)(2,1)S(1)} collective-permute-done((bf16[512,384]{1,0:T(8,128)(2,1)S(1)}, bf16[512,384]{1,0:T(8,128)(2,1)S(1)}, u32[]{:S(2)}, u32[]{:S(2)}) %collective-permute-start.2) | collective-permute-done | bytes 393248 | tf_op jit(solution)/shard_map/ppermute | solution.py:24
  223.9 2.2 collective-permute-done.1
  226.1 7.2 %collective-permute-done = bf16[512,384]{1,0:T(8,128)(2,1)S(1)} collective-permute-done((bf16[512,384]{1,0:T(8,128)(2,1)S(1)}, bf16[512,384]{1,0:T(8,128)(2,1)S(1)}, u32[]{:S(2)}, u32[]{:S(2)}) %collective-permute-start) | collective-permute-done | bytes 393248 | tf_op jit(solution)/shard_map/ppermute | solution.py:24
  233.3 4.4 %bitcast_convert_fusion.1 = bf16[512,1024]{1,0:T(8,128)(2,1)} fusion(bf16[1,512,384]{2,1,0:T(8,128)(2,1)S(1)} %bitcast.89, bf16[1,512,384]{2,1,0:T(8,128)(2,1)S(1)} %bitcast.90, bf16[1,512,384]{2,1,0:T(8,128)(2,1)S(1)} %bitcast.92, bf16[1,512,384]{2,1,0:T(8,128)(2,1)S(1)} %bitcast.87, bf16[1,384,1024]{2,1,0:T(8,128)(2,1)} %bitcast.16, ...), kind=kOutput, calls=%fused_computation.13 | convolution fusion | flops 1618214912 | bytes 5767168 | tf_op jit(solution)/shard_map/dot_general | solution.py:82
  237.7 2.3 reshape.214
  239.9 3.4 %copy.48 = bf16[4,64,2,1024]{3,2,0,1:T(2,128)(2,1)} copy(bf16[4,64,2,1024]{3,2,1,0:T(2,128)(2,1)} %reshape.214) | data formatting | bytes 2097152 | tf_op jit(solution)/shard_map/reshape | solution.py:85
  243.3 10.7 %all-to-all-start.1 = ((bf16[64,4,2,1024]{3,2,1,0:T(2,128)(2,1)}), bf16[64,4,2,1024]{3,2,1,0:T(2,128)(2,1)}, u32[]{:S(2)}, u32[]{:S(2)}) async-start(bf16[64,4,2,1024]{3,2,1,0:T(2,128)(2,1)} %bitcast.80), calls=%async_computation.1 | async-start | bytes 2097152 | tf_op jit(solution)/shard_map/all_to_all | solution.py:88
  254.2 0.3 select_reduce_fusion
  254.7 3.5 %convolution_bitcast_fusion = f32[64,1024]{1,0:T(8,128)} fusion(bf16[64,4,2,1024]{3,2,1,0:T(2,128)(2,1)} %all-to-all-done.3, s32[4,2]{1,0:T(4,128)S(1)} %iota_add_fusion, f32[64,64]{1,0:T(8,128)S(1)} %select_reduce_fusion, s32[64,64]{1,0:T(8,128)S(1)} %sub.20, pred[64,64]{1,0:T(8,128)(4,1)S(1)} %broadcast_compare_fusion), kind=kOutput, calls=%fused_computation.32 | convolution fusion | flops 201424896 | bytes 1347616 | tf_op jit(solution)/shard_map/dot_general | solution.py:95
  258.2 24.6 %all-to-all-done.1 = bf16[64,4,2,1024]{3,2,1,0:T(2,128)(2,1)} async-done(((bf16[64,4,2,1024]{3,2,1,0:T(2,128)(2,1)}), bf16[64,4,2,1024]{3,2,1,0:T(2,128)(2,1)}, u32[]{:S(2)}, u32[]{:S(2)}) %all-to-all-start.1) | async-done | bytes 1048608 | tf_op jit(solution)/shard_map/all_to_all | solution.py:88
  282.8 2.8 fusion.35
  285.9 8.8 %all_to_all.41 = bf16[4,4,4,1024]{3,2,1,0:T(4,128)(2,1)S(1)} all-to-all(bf16[4,4,4,1024]{3,2,1,0:T(4,128)(2,1)S(1)} %reshape.217), channel_id=1, replica_groups=mesh['dp'=4,'expert'=64] {'dp'}, dimensions={0} | all-to-all | bytes 262144 | tf_op jit(solution)/shard_map/all_to_all | solution.py:112
  294.7 0.7 copy.40
  (51 shorter events, 1.5 us)
Async XLA Ops:
  6.5 135.4 %copy-start = (bf16[1,4096,384]{2,1,0:T(8,128)(2,1)S(1)}, bf16[1,4096,384]{2,1,0:T(8,128)(2,1)}, u32[]{:S(2)}) copy-start(bf16[1,4096,384]{2,1,0:T(8,128)(2,1)} %param.15) | copy-start | bytes 9437188
  6.5 135.4 %all-gather.5.cloned.1.call-start = ((), (), s32[]{:S(2)}) async-start(), calls=%async_computation.6 | async-start | bytes 5242880 | tf_op jit(solution)/shard_map/all_gather | solution.py:77
  6.5 9.6 %copy-start.4 = (s32[16,4,8]{0,2,1:T(8,128)S(1)}, s32[16,4,8]{0,2,1:T(8,128)}, u32[]{:S(2)}) copy-start(s32[16,4,8]{0,2,1:T(8,128)} %param.10) | copy-start | bytes 6148
  6.5 10.3 %copy-start.5 = (s32[16]{0:T(128)S(1)}, s32[16]{0:T(128)}, u32[]{:S(2)}) copy-start(s32[16]{0:T(128)} %param.12) | copy-start | bytes 196
  10.3 20.9 %collective-permute-start.3 = (bf16[384,1024]{1,0:T(8,128)(2,1)}, bf16[384,1024]{1,0:T(8,128)(2,1)}, u32[]{:S(2)}, u32[]{:S(2)}) collective-permute-start(bf16[384,1024]{1,0:T(8,128)(2,1)} %get-tuple-element.16), channel_id=1, source_target_pairs={{0,64},{64,128},{128,192},{192,0},{1,65},{65,129},{129,193},{193,1... | collective-permute-start | bytes 2359304 | tf_op jit(solution)/shard_map/ppermute | solution.py:16
  11.9 37.3 %collective-permute-start.4 = (bf16[384,1024]{1,0:T(8,128)(2,1)}, bf16[384,1024]{1,0:T(8,128)(2,1)}, u32[]{:S(2)}, u32[]{:S(2)}) collective-permute-start(bf16[384,1024]{1,0:T(8,128)(2,1)} %get-tuple-element.18), channel_id=1, source_target_pairs={{0,128},{64,192},{128,0},{192,64},{1,129},{65,193},{129,1},{193,65... | collective-permute-start | bytes 2359304 | tf_op jit(solution)/shard_map/ppermute | solution.py:16
  14.8 34.4 %collective-permute-start.5 = (bf16[384,1024]{1,0:T(8,128)(2,1)}, bf16[384,1024]{1,0:T(8,128)(2,1)}, u32[]{:S(2)}, u32[]{:S(2)}) collective-permute-start(bf16[384,1024]{1,0:T(8,128)(2,1)} %get-tuple-element.15), channel_id=1, source_target_pairs={{0,192},{64,0},{128,64},{192,128},{1,193},{65,1},{129,65},{193,129... | collective-permute-start | bytes 2359304 | tf_op jit(solution)/shard_map/ppermute | solution.py:16
  95.0 109.8 %all-gather.3.cloned.1.call-start = ((), (), s32[]{:S(2)}) async-start(), calls=%async_computation.5 | async-start | bytes 5242880 | tf_op jit(solution)/shard_map/all_gather | solution.py:77
  142.0 4.7 %copy-start.7 = (bf16[512,4096]{1,0:T(8,128)(2,1)S(1)}, bf16[512,4096]{1,0:T(8,128)(2,1)}, u32[]{:S(2)}) copy-start(bf16[512,4096]{1,0:T(8,128)(2,1)} %all-gather.5.cloned.1.call-done) | copy-start | bytes 12582916
  142.0 4.7 %copy-start.8 = (bf16[1,4096,384]{2,1,0:T(8,128)(2,1)S(1)}, bf16[1,4096,384]{2,1,0:T(8,128)(2,1)}, u32[]{:S(2)}) copy-start(bf16[1,4096,384]{2,1,0:T(8,128)(2,1)} %param.16) | copy-start | bytes 9437188
  146.6 34.1 %copy-start.1 = (bf16[384,1024]{1,0:T(8,128)(2,1)S(1)}, bf16[384,1024]{1,0:T(8,128)(2,1)}, u32[]{:S(2)}) copy-start(bf16[384,1024]{1,0:T(8,128)(2,1)} %get-tuple-element.10) | copy-start | bytes 2359300
  149.0 12.8 %collective-permute-start.8 = (bf16[512,384]{1,0:T(8,128)(2,1)S(1)}, bf16[512,384]{1,0:T(8,128)(2,1)S(1)}, u32[]{:S(2)}, u32[]{:S(2)}) collective-permute-start(bf16[512,384]{1,0:T(8,128)(2,1)S(1)} %fusion.28), channel_id=1, source_target_pairs={{0,192},{64,0},{128,64},{192,128},{1,193},{65,1},{129,65},{193,129... | collective-permute-start | bytes 1179656 | tf_op jit(solution)/shard_map/ppermute | solution.py:24
  150.2 16.1 %collective-permute-start.7 = (bf16[512,384]{1,0:T(8,128)(2,1)S(1)}, bf16[512,384]{1,0:T(8,128)(2,1)S(1)}, u32[]{:S(2)}, u32[]{:S(2)}) collective-permute-start(bf16[512,384]{1,0:T(8,128)(2,1)S(1)} %fusion.28), channel_id=1, source_target_pairs={{0,128},{64,192},{128,0},{192,64},{1,129},{65,193},{129,1},{193,65... | collective-permute-start | bytes 1179656 | tf_op jit(solution)/shard_map/ppermute | solution.py:24
  152.0 28.7 %collective-permute-start.6 = (bf16[512,384]{1,0:T(8,128)(2,1)S(1)}, bf16[512,384]{1,0:T(8,128)(2,1)S(1)}, u32[]{:S(2)}, u32[]{:S(2)}) collective-permute-start(bf16[512,384]{1,0:T(8,128)(2,1)S(1)} %fusion.28), channel_id=1, source_target_pairs={{0,64},{64,128},{128,192},{192,0},{1,65},{65,129},{129,193},{193,1... | collective-permute-start | bytes 1179656 | tf_op jit(solution)/shard_map/ppermute | solution.py:24
  190.8 52.5 %all-to-all-start.3 = ((bf16[64,4,2,1024]{3,2,1,0:T(2,128)(2,1)}), bf16[64,4,2,1024]{3,2,1,0:T(2,128)(2,1)}, u32[]{:S(2)}, u32[]{:S(2)}) async-start(bf16[64,4,2,1024]{3,2,1,0:T(2,128)(2,1)} %bitcast.79), calls=%async_computation.3 | async-start | bytes 2097152 | tf_op jit(solution)/shard_map/all_to_all | solution.py:88
  204.8 4.7 %copy-start.6 = (bf16[512,4096]{1,0:T(8,128)(2,1)S(1)}, bf16[512,4096]{1,0:T(8,128)(2,1)}, u32[]{:S(2)}) copy-start(bf16[512,4096]{1,0:T(8,128)(2,1)} %all-gather.3.cloned.1.call-done) | copy-start | bytes 12582916
  204.8 4.7 %copy-start.9 = (bf16[1,4096,384]{2,1,0:T(8,128)(2,1)S(1)}, bf16[1,4096,384]{2,1,0:T(8,128)(2,1)}, u32[]{:S(2)}) copy-start(bf16[1,4096,384]{2,1,0:T(8,128)(2,1)} %param.16) | copy-start | bytes 9437188
  209.5 23.8 %copy-start.2 = (bf16[384,1024]{1,0:T(8,128)(2,1)S(1)}, bf16[384,1024]{1,0:T(8,128)(2,1)}, u32[]{:S(2)}) copy-start(bf16[384,1024]{1,0:T(8,128)(2,1)} %get-tuple-element.10) | copy-start | bytes 2359300
  211.8 12.0 %collective-permute-start.2 = (bf16[512,384]{1,0:T(8,128)(2,1)S(1)}, bf16[512,384]{1,0:T(8,128)(2,1)S(1)}, u32[]{:S(2)}, u32[]{:S(2)}) collective-permute-start(bf16[512,384]{1,0:T(8,128)(2,1)S(1)} %fusion.31), channel_id=1, source_target_pairs={{0,192},{64,0},{128,64},{192,128},{1,193},{65,1},{129,65},{193,129... | collective-permute-start | bytes 1179656 | tf_op jit(solution)/shard_map/ppermute | solution.py:24
  212.5 13.6 %collective-permute-start.1 = (bf16[512,384]{1,0:T(8,128)(2,1)S(1)}, bf16[512,384]{1,0:T(8,128)(2,1)S(1)}, u32[]{:S(2)}, u32[]{:S(2)}) collective-permute-start(bf16[512,384]{1,0:T(8,128)(2,1)S(1)} %fusion.31), channel_id=1, source_target_pairs={{0,128},{64,192},{128,0},{192,64},{1,129},{65,193},{129,1},{193,65... | collective-permute-start | bytes 1179656 | tf_op jit(solution)/shard_map/ppermute | solution.py:24
  214.3 18.9 %collective-permute-start = (bf16[512,384]{1,0:T(8,128)(2,1)S(1)}, bf16[512,384]{1,0:T(8,128)(2,1)S(1)}, u32[]{:S(2)}, u32[]{:S(2)}) collective-permute-start(bf16[512,384]{1,0:T(8,128)(2,1)S(1)} %fusion.31), channel_id=1, source_target_pairs={{0,64},{64,128},{128,192},{192,0},{1,65},{65,129},{129,193},{193,1... | collective-permute-start | bytes 1179656 | tf_op jit(solution)/shard_map/ppermute | solution.py:24
  237.7 16.4 %copy-start.3 = (f32[16,4,8]{0,2,1:T(8,128)S(1)}, f32[16,4,8]{0,2,1:T(8,128)}, u32[]{:S(2)}) copy-start(f32[16,4,8]{0,2,1:T(8,128)} %param.11) | copy-start | bytes 6148
  237.7 16.8 %copy-start.10 = (s32[16]{0:T(128)S(1)}, s32[16]{0:T(128)}, u32[]{:S(2)}) copy-start(s32[16]{0:T(128)} %param.14) | copy-start | bytes 196
  243.3 39.5 %all-to-all-start.1 = ((bf16[64,4,2,1024]{3,2,1,0:T(2,128)(2,1)}), bf16[64,4,2,1024]{3,2,1,0:T(2,128)(2,1)}, u32[]{:S(2)}, u32[]{:S(2)}) async-start(bf16[64,4,2,1024]{3,2,1,0:T(2,128)(2,1)} %bitcast.80), calls=%async_computation.1 | async-start | bytes 2097152 | tf_op jit(solution)/shard_map/all_to_all | solution.py:88
Sparse Core Ops, SparseCore 0:
  95.1 46.8 all-gather.4
  143.8 60.9 all-gather.2
where the time goes:
time: 303 us; the launch traced here: 302 us
  waiting for transfers between devices  106 us (35%)
  blocking collectives  84.3 us (28%)
  matrix products  34.3 us (11%)
  starting transfers between devices  34.2 us (11%)
  local copies, waits for them, and re-layouts  28 us (9%)
  between operations  14.3 us (5%)
    all_to_all x2, blocking collectives, body(): lax.all_to_all(outgoing, 'expert', split_axis=0, concat_axis=0, tiled=True)  75.5 us
    ppermute x6, waiting for transfers between devices, exchange_all(): pieces.append(lax.ppermute(block, 'dp', pairs))  46.3 us
    ppermute x3, waiting for transfers between devices, exchange_gather(): pieces.append(lax.ppermute(outgoing, 'dp', pairs))  27 us
    all_to_all x2, waiting for transfers between devices, body(): lax.all_to_all(by_source, 'expert', split_axis=0, concat_axis=0, tiled=True)  24.6 us
    all_to_all x2, starting transfers between devices, body(): lax.all_to_all(by_source, 'expert', split_axis=0, concat_axis=0, tiled=True)  21.5 us
    reshape x4, local copies, waits for them, and re-layouts, body(): expert_cols.reshape(replica_count, expert_count, sub, columns)  11.2 us
    all_to_all x4, local copies, waits for them, and re-layouts, body(): lax.all_to_all(outgoing, 'expert', split_axis=0, concat_axis=0, tiled=True)  9.66 us
    dot_general x2, matrix products, body(): gate_part = jnp.dot(gathered, w_gate[0], preferred_element_type=jnp.float32)  9.32 us
  transfers between devices with their start and end apart: 13, of which 11 were waited for; matrix products, arithmetic and copies ran while one was open for 15% of the time, Pallas kernels for 0%

commit v1 on v0

--- a/solution.py
+++ b/solution.py
@@ -74,7 +74,9 @@
     for chunk in range(chunks):
         outgoing = outgoings[chunk]
         arrived = lax.all_to_all(outgoing, "expert", split_axis=0, concat_axis=0, tiled=True)
-        gathered = lax.all_gather(arrived, "dp", axis=0, tiled=True)
+        gathered = jnp.concatenate(
+            lax.all_to_all(jnp.stack([arrived] * lax.axis_size("dp")), "dp", 0, 0), axis=0
+        )
         gate_part = jnp.dot(gathered, w_gate[0], preferred_element_type=jnp.float32)
         up_part = jnp.dot(gathered, w_up[0], preferred_element_type=jnp.float32)
         activated = (jax.nn.silu(gate_part) * up_part).astype(jnp.bfloat16)

time: 303 us -> 363 us (1.20)
  waiting for transfers between devices: 106 us -> 216 us
  blocking collectives: 84.3 us -> 8.51 us
  starting transfers between devices: 34.2 us -> 60.2 us
  between operations: 14.3 us -> 0.93 us
  local copies, waits for them, and re-layouts: 28 us -> 35.5 us
  matrix products: 34.3 us -> 38.9 us
    all_to_all x0 -> x4, waiting for transfers between devices: none -> 96 us  [the longest x2 50.1 us: body(): lax.all_to_all(outgoing, 'expert', split_axis=0, concat_axis=0, tiled=True)]
    all_to_all x2 -> x0, blocking collectives: 75.5 us -> none  [body(): lax.all_to_all(outgoing, 'expert', split_axis=0, concat_axis=0, tiled=True)]
    all_to_all x0 -> x4, starting transfers between devices: none -> 27.8 us  [the longest x2 18 us: body(): lax.all_to_all(outgoing, 'expert', split_axis=0, concat_axis=0, tiled=True)]
    ppermute x6, waiting for transfers between devices: 46.3 us -> 68.7 us  [exchange_all(): pieces.append(lax.ppermute(block, 'dp', pairs))]
    another operation x0 -> x4, local copies, waits for them, and re-layouts: none -> 11.9 us  [body(): jnp.stack([arrived] * lax.axis_size('dp'))]
    all_gather x2 -> x0, waiting for transfers between devices: 8.25 us -> none  [body(): gathered = lax.all_gather(arrived, 'dp', axis=0, tiled=True)]
    all_to_all x4 -> x2, local copies, waits for them, and re-layouts: 9.66 us -> 5.07 us  [body(): lax.all_to_all(outgoing, 'expert', split_axis=0, concat_axis=0, tiled=True)]
    dot_general x2, matrix products: 4.69 us -> 9.26 us  [body(): up_part = jnp.dot(gathered, w_up[0], preferred_element_type=jnp.float32)]
  transfers between devices with their start and end apart: 13 -> 15, of which waited for: 11 -> 12; matrix products, arithmetic and copies ran while one was open for 15% -> 15% of each run, Pallas kernels for 0% -> 0%
where the time goes in v1:
time: 363 us; the launch traced here: 361 us
  waiting for transfers between devices  216 us (60%)
  starting transfers between devices  60.2 us (17%)
  matrix products  38.9 us (11%)
  local copies, waits for them, and re-layouts  35.5 us (10%)
  blocking collectives  8.51 us (2%)
    ppermute x6, waiting for transfers between devices, exchange_all(): pieces.append(lax.ppermute(block, 'dp', pairs))  68.7 us
    all_to_all x2, waiting for transfers between devices, body(): lax.all_to_all(outgoing, 'expert', split_axis=0, concat_axis=0, tiled=True)  50.1 us
    all_to_all x2, waiting for transfers between devices, body(): lax.all_to_all(jnp.stack([arrived] * lax.axis_size('dp')), 'dp', 0, 0)  45.9 us
    ppermute x3, waiting for transfers between devices, exchange_gather(): pieces.append(lax.ppermute(outgoing, 'dp', pairs))  27 us
    all_to_all x2, waiting for transfers between devices, body(): lax.all_to_all(by_source, 'expert', split_axis=0, concat_axis=0, tiled=True)  24.6 us
    all_to_all x2, starting transfers between devices, body(): lax.all_to_all(by_source, 'expert', split_axis=0, concat_axis=0, tiled=True)  18.5 us
    all_to_all x2, starting transfers between devices, body(): lax.all_to_all(outgoing, 'expert', split_axis=0, concat_axis=0, tiled=True)  18 us
    another operation x4, local copies, waits for them, and re-layouts, body(): jnp.stack([arrived] * lax.axis_size('dp'))  11.9 us
  transfers between devices with their start and end apart: 15, of which 12 were waited for; matrix products, arithmetic and copies ran while one was open for 15% of the time, Pallas kernels for 0%

profile of v1, /device:TPU:2, one launch (start us, length us, event | category | flops | bytes accessed | tf_op | source)
XLA Modules:
  0.0 361.5 jit_solution(16574425634818592104)
XLA Ops:
  0.0 3.7 %dynamic-slice_bitcast_fusion = (bf16[384,1024]{1,0:T(8,128)(2,1)}, bf16[384,1024]{1,0:T(8,128)(2,1)}, bf16[384,1024]{1,0:T(8,128)(2,1)}, bf16[384,1024]{1,0:T(8,128)(2,1)}) fusion(bf16[1,384,4096]{2,1,0:T(8,128)(2,1)} %param.17, s32[]{:T(128)S(6)} %select_n.63, s32[]{:T(128)S(6)} %select_n.59, s32[]{:T(128)S(6)} %select_n.57, s32[]{:T(128)S(6)} %select_n.61), kind=kLoop, calls=%fused_computation.40 | loop fusion | bytes 6291472 | tf_op jit(solution)/shard_map/dynamic_slice | solution.py:14
  3.7 1.6 collective-permute-start.3
  5.3 2.9 collective-permute-start.4
  8.2 1.3 collective-permute-start.5
  11.2 2.0 reshape.225
  13.2 2.4 convolution_convert_fusion
  15.6 9.0 %collective-permute-done.3 = bf16[384,1024]{1,0:T(8,128)(2,1)} collective-permute-done((bf16[384,1024]{1,0:T(8,128)(2,1)}, bf16[384,1024]{1,0:T(8,128)(2,1)}, u32[]{:S(2)}, u32[]{:S(2)}) %collective-permute-start.3) | collective-permute-done | bytes 786464 | tf_op jit(solution)/shard_map/ppermute | solution.py:16
  24.6 18.0 %collective-permute-done.4 = bf16[384,1024]{1,0:T(8,128)(2,1)} collective-permute-done((bf16[384,1024]{1,0:T(8,128)(2,1)}, bf16[384,1024]{1,0:T(8,128)(2,1)}, u32[]{:S(2)}, u32[]{:S(2)}) %collective-permute-start.4) | collective-permute-done | bytes 786464 | tf_op jit(solution)/shard_map/ppermute | solution.py:16
  42.6 2.5 all_to_all.31
  45.2 12.2 %all-to-all-start.3 = ((bf16[64,2,4096]{2,1,0:T(2,128)(2,1)}), bf16[64,2,4096]{2,1,0:T(2,128)(2,1)}, u32[]{:S(2)}, u32[]{:S(2)}) async-start(bf16[64,2,4096]{2,1,0:T(2,128)(2,1)} %all_to_all.31), calls=%async_computation.3 | async-start | bytes 2097152 | tf_op jit(solution)/shard_map/all_to_all | solution.py:76
  57.4 2.4 convolution_convert_fusion.1
  59.9 2.5 all_to_all.27
  62.4 23.7 %all-to-all-done.3 = bf16[64,2,4096]{2,1,0:T(2,128)(2,1)} async-done(((bf16[64,2,4096]{2,1,0:T(2,128)(2,1)}), bf16[64,2,4096]{2,1,0:T(2,128)(2,1)}, u32[]{:S(2)}, u32[]{:S(2)}) %all-to-all-start.3) | async-done | bytes 1048608 | tf_op jit(solution)/shard_map/all_to_all | solution.py:76
  86.1 5.8 %all-to-all-start = ((bf16[64,2,4096]{2,1,0:T(2,128)(2,1)}), bf16[64,2,4096]{2,1,0:T(2,128)(2,1)}, u32[]{:S(2)}, u32[]{:S(2)}) async-start(bf16[64,2,4096]{2,1,0:T(2,128)(2,1)} %all_to_all.27), calls=%async_computation | async-start | bytes 2097152 | tf_op jit(solution)/shard_map/all_to_all | solution.py:76
  92.0 2.3 stack.75
  94.2 26.4 %all-to-all-done = bf16[64,2,4096]{2,1,0:T(2,128)(2,1)} async-done(((bf16[64,2,4096]{2,1,0:T(2,128)(2,1)}), bf16[64,2,4096]{2,1,0:T(2,128)(2,1)}, u32[]{:S(2)}, u32[]{:S(2)}) %all-to-all-start) | async-done | bytes 1048608 | tf_op jit(solution)/shard_map/all_to_all | solution.py:76
  120.7 3.7 %stack.76 = bf16[4,128,4096]{2,1,0:T(8,128)(2,1)} broadcast(bf16[128,4096]{1,0:T(8,128)(2,1)} %stack.75), dimensions={1,2} | broadcast | bytes 5242880 | tf_op jit(solution)/shard_map/stack | solution.py:78
  124.3 4.9 %all-to-all-start.4 = ((bf16[4,128,4096]{2,1,0:T(8,128)(2,1)}), bf16[4,128,4096]{2,1,0:T(8,128)(2,1)}, u32[]{:S(2)}, u32[]{:S(2)}) async-start(bf16[4,128,4096]{2,1,0:T(8,128)(2,1)} %stack.76), calls=%async_computation.4 | async-start | bytes 8388608 | tf_op jit(solution)/shard_map/all_to_all | solution.py:78
  129.3 2.3 stack.63
  131.6 45.9 %all-to-all-done.4 = bf16[4,128,4096]{2,1,0:T(8,128)(2,1)} async-done(((bf16[4,128,4096]{2,1,0:T(8,128)(2,1)}), bf16[4,128,4096]{2,1,0:T(8,128)(2,1)}, u32[]{:S(2)}, u32[]{:S(2)}) %all-to-all-start.4) | async-done | bytes 4194336 | tf_op jit(solution)/shard_map/all_to_all | solution.py:78
  177.4 3.7 %stack.64 = bf16[4,128,4096]{2,1,0:T(8,128)(2,1)} broadcast(bf16[128,4096]{1,0:T(8,128)(2,1)} %stack.63), dimensions={1,2} | broadcast | bytes 5242880 | tf_op jit(solution)/shard_map/stack | solution.py:78
  181.2 4.9 %all-to-all-start.1 = ((bf16[4,128,4096]{2,1,0:T(8,128)(2,1)}), bf16[4,128,4096]{2,1,0:T(8,128)(2,1)}, u32[]{:S(2)}, u32[]{:S(2)}) async-start(bf16[4,128,4096]{2,1,0:T(8,128)(2,1)} %stack.64), calls=%async_computation.1 | async-start | bytes 8388608 | tf_op jit(solution)/shard_map/all_to_all | solution.py:78
  186.0 4.7 %fusion.4 = f32[512,384]{1,0:T(8,128)S(1)} fusion(bf16[512,4096]{1,0:T(8,128)(2,1)} %bitcast.22, bf16[1,4096,384]{2,1,0:T(8,128)(2,1)S(1)} %copy-done), kind=kOutput, calls=%fused_computation.8 | convolution fusion | flops 1610612736 | bytes 8126464 | tf_op jit(solution)/shard_map/dot_general | solution.py:80
  190.7 4.6 %fusion.28 = bf16[512,384]{1,0:T(8,128)(2,1)S(1)} fusion(bf16[512,4096]{1,0:T(8,128)(2,1)} %bitcast.22, bf16[1,4096,384]{2,1,0:T(8,128)(2,1)S(1)} %copy-done.6, f32[512,384]{1,0:T(8,128)S(1)} %fusion.4), kind=kOutput, calls=%fused_computation.30 | convolution fusion | flops 1611792384 | bytes 8519680 | tf_op jit(solution)/shard_map/dot_general | solution.py:81
  195.4 3.3 collective-permute-start.8
  199.5 0.9 collective-permute-start.6
  200.3 42.9 %collective-permute-done.8 = bf16[512,384]{1,0:T(8,128)(2,1)S(1)} collective-permute-done((bf16[512,384]{1,0:T(8,128)(2,1)S(1)}, bf16[512,384]{1,0:T(8,128)(2,1)S(1)}, u32[]{:S(2)}, u32[]{:S(2)}) %collective-permute-start.8) | collective-permute-done | bytes 393248 | tf_op jit(solution)/shard_map/ppermute | solution.py:24
  243.2 1.5 collective-permute-done.7
  244.7 5.0 %collective-permute-done.6 = bf16[512,384]{1,0:T(8,128)(2,1)S(1)} collective-permute-done((bf16[512,384]{1,0:T(8,128)(2,1)S(1)}, bf16[512,384]{1,0:T(8,128)(2,1)S(1)}, u32[]{:S(2)}, u32[]{:S(2)}) %collective-permute-start.6) | collective-permute-done | bytes 393248 | tf_op jit(solution)/shard_map/ppermute | solution.py:24
  249.7 4.5 %bitcast_convert_fusion = bf16[512,1024]{1,0:T(8,128)(2,1)} fusion(bf16[1,512,384]{2,1,0:T(8,128)(2,1)S(1)} %bitcast.93, bf16[1,512,384]{2,1,0:T(8,128)(2,1)S(1)} %bitcast.95, bf16[1,512,384]{2,1,0:T(8,128)(2,1)S(1)} %bitcast.96, bf16[1,512,384]{2,1,0:T(8,128)(2,1)S(1)} %bitcast.90, bf16[1,384,1024]{2,1,0:T(8,128)(2,1)} %bitcast.17, ...), kind=kOutput, calls=%fused_computation.12 | convolution fusion | flops 1618214912 | bytes 5767168 | tf_op jit(solution)/shard_map/dot_general | solution.py:84
  254.2 2.3 reshape.229
  256.5 3.5 copy.47
  260.0 8.1 %all-to-all-start.5 = ((bf16[64,4,2,1024]{3,2,1,0:T(2,128)(2,1)}), bf16[64,4,2,1024]{3,2,1,0:T(2,128)(2,1)}, u32[]{:S(2)}, u32[]{:S(2)}) async-start(bf16[64,4,2,1024]{3,2,1,0:T(2,128)(2,1)} %bitcast.81), calls=%async_computation.5 | async-start | bytes 2097152 | tf_op jit(solution)/shard_map/all_to_all | solution.py:90
  268.0 4.7 %fusion.6 = f32[512,384]{1,0:T(8,128)S(1)} fusion(bf16[512,4096]{1,0:T(8,128)(2,1)} %bitcast.3, bf16[1,4096,384]{2,1,0:T(8,128)(2,1)S(1)} %copy-done), kind=kOutput, calls=%fused_computation.10 | convolution fusion | flops 1610612736 | bytes 8126464 | tf_op jit(solution)/shard_map/dot_general | solution.py:80
  272.7 4.6 %fusion.31 = bf16[512,384]{1,0:T(8,128)(2,1)S(1)} fusion(bf16[512,4096]{1,0:T(8,128)(2,1)} %bitcast.3, bf16[1,4096,384]{2,1,0:T(8,128)(2,1)S(1)} %copy-done.7, f32[512,384]{1,0:T(8,128)S(1)} %fusion.6), kind=kOutput, calls=%fused_computation.31 | convolution fusion | flops 1611792384 | bytes 8519680 | tf_op jit(solution)/shard_map/dot_general | solution.py:81
  277.4 1.6 collective-permute-start.2
  279.0 1.5 collective-permute-start.1
  280.4 9.0 %collective-permute-done.2 = bf16[512,384]{1,0:T(8,128)(2,1)S(1)} collective-permute-done((bf16[512,384]{1,0:T(8,128)(2,1)S(1)}, bf16[512,384]{1,0:T(8,128)(2,1)S(1)}, u32[]{:S(2)}, u32[]{:S(2)}) %collective-permute-start.2) | collective-permute-done | bytes 393248 | tf_op jit(solution)/shard_map/ppermute | solution.py:24
  289.4 3.1 collective-permute-done.1
  292.5 7.3 %collective-permute-done = bf16[512,384]{1,0:T(8,128)(2,1)S(1)} collective-permute-done((bf16[512,384]{1,0:T(8,128)(2,1)S(1)}, bf16[512,384]{1,0:T(8,128)(2,1)S(1)}, u32[]{:S(2)}, u32[]{:S(2)}) %collective-permute-start) | collective-permute-done | bytes 393248 | tf_op jit(solution)/shard_map/ppermute | solution.py:24
  299.8 4.4 %bitcast_convert_fusion.1 = bf16[512,1024]{1,0:T(8,128)(2,1)} fusion(bf16[1,512,384]{2,1,0:T(8,128)(2,1)S(1)} %bitcast.91, bf16[1,512,384]{2,1,0:T(8,128)(2,1)S(1)} %bitcast.92, bf16[1,512,384]{2,1,0:T(8,128)(2,1)S(1)} %bitcast.94, bf16[1,512,384]{2,1,0:T(8,128)(2,1)S(1)} %bitcast.89, bf16[1,384,1024]{2,1,0:T(8,128)(2,1)} %bitcast.17, ...), kind=kOutput, calls=%fused_computation.13 | convolution fusion | flops 1618214912 | bytes 5767168 | tf_op jit(solution)/shard_map/dot_general | solution.py:84
  304.2 2.3 reshape.227
  306.5 3.4 copy.48
  309.9 10.5 %all-to-all-start.2 = ((bf16[64,4,2,1024]{3,2,1,0:T(2,128)(2,1)}), bf16[64,4,2,1024]{3,2,1,0:T(2,128)(2,1)}, u32[]{:S(2)}, u32[]{:S(2)}) async-start(bf16[64,4,2,1024]{3,2,1,0:T(2,128)(2,1)} %bitcast.82), calls=%async_computation.2 | async-start | bytes 2097152 | tf_op jit(solution)/shard_map/all_to_all | solution.py:90
  321.0 3.5 convolution_bitcast_fusion
  324.5 24.6 %all-to-all-done.2 = bf16[64,4,2,1024]{3,2,1,0:T(2,128)(2,1)} async-done(((bf16[64,4,2,1024]{3,2,1,0:T(2,128)(2,1)}), bf16[64,4,2,1024]{3,2,1,0:T(2,128)(2,1)}, u32[]{:S(2)}, u32[]{:S(2)}) %all-to-all-start.2) | async-done | bytes 1048608 | tf_op jit(solution)/shard_map/all_to_all | solution.py:90
  349.1 2.8 fusion.35
  352.3 8.5 %all_to_all.43 = bf16[4,4,4,1024]{3,2,1,0:T(4,128)(2,1)S(1)} all-to-all(bf16[4,4,4,1024]{3,2,1,0:T(4,128)(2,1)S(1)} %reshape.231), channel_id=1, replica_groups=mesh['dp'=4,'expert'=64] {'dp'}, dimensions={0} | all-to-all | bytes 262144 | tf_op jit(solution)/shard_map/all_to_all | solution.py:114
  (49 shorter events, 3.5 us)
Async XLA Ops:
  0.0 186.0 %copy-start = (bf16[1,4096,384]{2,1,0:T(8,128)(2,1)S(1)}, bf16[1,4096,384]{2,1,0:T(8,128)(2,1)}, u32[]{:S(2)}) copy-start(bf16[1,4096,384]{2,1,0:T(8,128)(2,1)} %param.15) | copy-start | bytes 9437188
  0.0 9.5 %copy-start.4 = (s32[16,4,8]{0,2,1:T(8,128)S(1)}, s32[16,4,8]{0,2,1:T(8,128)}, u32[]{:S(2)}) copy-start(s32[16,4,8]{0,2,1:T(8,128)} %param.10) | copy-start | bytes 6148
  0.0 10.3 %copy-start.5 = (s32[16]{0:T(128)S(1)}, s32[16]{0:T(128)}, u32[]{:S(2)}) copy-start(s32[16]{0:T(128)} %param.12) | copy-start | bytes 196
  3.7 20.9 %collective-permute-start.3 = (bf16[384,1024]{1,0:T(8,128)(2,1)}, bf16[384,1024]{1,0:T(8,128)(2,1)}, u32[]{:S(2)}, u32[]{:S(2)}) collective-permute-start(bf16[384,1024]{1,0:T(8,128)(2,1)} %get-tuple-element.16), channel_id=1, source_target_pairs={{0,64},{64,128},{128,192},{192,0},{1,65},{65,129},{129,193},{193,1... | collective-permute-start | bytes 2359304 | tf_op jit(solution)/shard_map/ppermute | solution.py:16
  5.3 37.3 %collective-permute-start.4 = (bf16[384,1024]{1,0:T(8,128)(2,1)}, bf16[384,1024]{1,0:T(8,128)(2,1)}, u32[]{:S(2)}, u32[]{:S(2)}) collective-permute-start(bf16[384,1024]{1,0:T(8,128)(2,1)} %get-tuple-element.18), channel_id=1, source_target_pairs={{0,128},{64,192},{128,0},{192,64},{1,129},{65,193},{129,1},{193,65... | collective-permute-start | bytes 2359304 | tf_op jit(solution)/shard_map/ppermute | solution.py:16
  8.2 34.4 %collective-permute-start.5 = (bf16[384,1024]{1,0:T(8,128)(2,1)}, bf16[384,1024]{1,0:T(8,128)(2,1)}, u32[]{:S(2)}, u32[]{:S(2)}) collective-permute-start(bf16[384,1024]{1,0:T(8,128)(2,1)} %get-tuple-element.15), channel_id=1, source_target_pairs={{0,192},{64,0},{128,64},{192,128},{1,193},{65,1},{129,65},{193,129... | collective-permute-start | bytes 2359304 | tf_op jit(solution)/shard_map/ppermute | solution.py:16
  45.2 40.9 %all-to-all-start.3 = ((bf16[64,2,4096]{2,1,0:T(2,128)(2,1)}), bf16[64,2,4096]{2,1,0:T(2,128)(2,1)}, u32[]{:S(2)}, u32[]{:S(2)}) async-start(bf16[64,2,4096]{2,1,0:T(2,128)(2,1)} %all_to_all.31), calls=%async_computation.3 | async-start | bytes 2097152 | tf_op jit(solution)/shard_map/all_to_all | solution.py:76
  86.1 34.6 %all-to-all-start = ((bf16[64,2,4096]{2,1,0:T(2,128)(2,1)}), bf16[64,2,4096]{2,1,0:T(2,128)(2,1)}, u32[]{:S(2)}, u32[]{:S(2)}) async-start(bf16[64,2,4096]{2,1,0:T(2,128)(2,1)} %all_to_all.27), calls=%async_computation | async-start | bytes 2097152 | tf_op jit(solution)/shard_map/all_to_all | solution.py:76
  124.3 53.1 %all-to-all-start.4 = ((bf16[4,128,4096]{2,1,0:T(8,128)(2,1)}), bf16[4,128,4096]{2,1,0:T(8,128)(2,1)}, u32[]{:S(2)}, u32[]{:S(2)}) async-start(bf16[4,128,4096]{2,1,0:T(8,128)(2,1)} %stack.76), calls=%async_computation.4 | async-start | bytes 8388608 | tf_op jit(solution)/shard_map/all_to_all | solution.py:78
  181.2 78.8 %all-to-all-start.1 = ((bf16[4,128,4096]{2,1,0:T(8,128)(2,1)}), bf16[4,128,4096]{2,1,0:T(8,128)(2,1)}, u32[]{:S(2)}, u32[]{:S(2)}) async-start(bf16[4,128,4096]{2,1,0:T(8,128)(2,1)} %stack.64), calls=%async_computation.1 | async-start | bytes 8388608 | tf_op jit(solution)/shard_map/all_to_all | solution.py:78
  186.0 4.7 %copy-start.6 = (bf16[1,4096,384]{2,1,0:T(8,128)(2,1)S(1)}, bf16[1,4096,384]{2,1,0:T(8,128)(2,1)}, u32[]{:S(2)}) copy-start(bf16[1,4096,384]{2,1,0:T(8,128)(2,1)} %param.16) | copy-start | bytes 9437188
  190.7 59.0 %copy-start.1 = (bf16[384,1024]{1,0:T(8,128)(2,1)S(1)}, bf16[384,1024]{1,0:T(8,128)(2,1)}, u32[]{:S(2)}) copy-start(bf16[384,1024]{1,0:T(8,128)(2,1)} %get-tuple-element.10) | copy-start | bytes 2359300
  195.4 47.9 %collective-permute-start.8 = (bf16[512,384]{1,0:T(8,128)(2,1)S(1)}, bf16[512,384]{1,0:T(8,128)(2,1)S(1)}, u32[]{:S(2)}, u32[]{:S(2)}) collective-permute-start(bf16[512,384]{1,0:T(8,128)(2,1)S(1)} %fusion.28), channel_id=1, source_target_pairs={{0,192},{64,0},{128,64},{192,128},{1,193},{65,1},{129,65},{193,129... | collective-permute-start | bytes 1179656 | tf_op jit(solution)/shard_map/ppermute | solution.py:24
  198.6 46.1 %collective-permute-start.7 = (bf16[512,384]{1,0:T(8,128)(2,1)S(1)}, bf16[512,384]{1,0:T(8,128)(2,1)S(1)}, u32[]{:S(2)}, u32[]{:S(2)}) collective-permute-start(bf16[512,384]{1,0:T(8,128)(2,1)S(1)} %fusion.28), channel_id=1, source_target_pairs={{0,128},{64,192},{128,0},{192,64},{1,129},{65,193},{129,1},{193,65... | collective-permute-start | bytes 1179656 | tf_op jit(solution)/shard_map/ppermute | solution.py:24
  199.5 50.2 %collective-permute-start.6 = (bf16[512,384]{1,0:T(8,128)(2,1)S(1)}, bf16[512,384]{1,0:T(8,128)(2,1)S(1)}, u32[]{:S(2)}, u32[]{:S(2)}) collective-permute-start(bf16[512,384]{1,0:T(8,128)(2,1)S(1)} %fusion.28), channel_id=1, source_target_pairs={{0,64},{64,128},{128,192},{192,0},{1,65},{65,129},{129,193},{193,1... | collective-permute-start | bytes 1179656 | tf_op jit(solution)/shard_map/ppermute | solution.py:24
  260.0 49.9 %all-to-all-start.5 = ((bf16[64,4,2,1024]{3,2,1,0:T(2,128)(2,1)}), bf16[64,4,2,1024]{3,2,1,0:T(2,128)(2,1)}, u32[]{:S(2)}, u32[]{:S(2)}) async-start(bf16[64,4,2,1024]{3,2,1,0:T(2,128)(2,1)} %bitcast.81), calls=%async_computation.5 | async-start | bytes 2097152 | tf_op jit(solution)/shard_map/all_to_all | solution.py:90
  268.0 4.7 %copy-start.7 = (bf16[1,4096,384]{2,1,0:T(8,128)(2,1)S(1)}, bf16[1,4096,384]{2,1,0:T(8,128)(2,1)}, u32[]{:S(2)}) copy-start(bf16[1,4096,384]{2,1,0:T(8,128)(2,1)} %param.16) | copy-start | bytes 9437188
  272.7 27.1 %copy-start.2 = (bf16[384,1024]{1,0:T(8,128)(2,1)S(1)}, bf16[384,1024]{1,0:T(8,128)(2,1)}, u32[]{:S(2)}) copy-start(bf16[384,1024]{1,0:T(8,128)(2,1)} %get-tuple-element.10) | copy-start | bytes 2359300
  277.4 12.0 %collective-permute-start.2 = (bf16[512,384]{1,0:T(8,128)(2,1)S(1)}, bf16[512,384]{1,0:T(8,128)(2,1)S(1)}, u32[]{:S(2)}, u32[]{:S(2)}) collective-permute-start(bf16[512,384]{1,0:T(8,128)(2,1)S(1)} %fusion.31), channel_id=1, source_target_pairs={{0,192},{64,0},{128,64},{192,128},{1,193},{65,1},{129,65},{193,129... | collective-permute-start | bytes 1179656 | tf_op jit(solution)/shard_map/ppermute | solution.py:24
  279.0 13.5 %collective-permute-start.1 = (bf16[512,384]{1,0:T(8,128)(2,1)S(1)}, bf16[512,384]{1,0:T(8,128)(2,1)S(1)}, u32[]{:S(2)}, u32[]{:S(2)}) collective-permute-start(bf16[512,384]{1,0:T(8,128)(2,1)S(1)} %fusion.31), channel_id=1, source_target_pairs={{0,128},{64,192},{128,0},{192,64},{1,129},{65,193},{129,1},{193,65... | collective-permute-start | bytes 1179656 | tf_op jit(solution)/shard_map/ppermute | solution.py:24
  280.4 19.4 %collective-permute-start = (bf16[512,384]{1,0:T(8,128)(2,1)S(1)}, bf16[512,384]{1,0:T(8,128)(2,1)S(1)}, u32[]{:S(2)}, u32[]{:S(2)}) collective-permute-start(bf16[512,384]{1,0:T(8,128)(2,1)S(1)} %fusion.31), channel_id=1, source_target_pairs={{0,64},{64,128},{128,192},{192,0},{1,65},{65,129},{129,193},{193,1... | collective-permute-start | bytes 1179656 | tf_op jit(solution)/shard_map/ppermute | solution.py:24
  304.2 16.1 %copy-start.3 = (f32[16,4,8]{0,2,1:T(8,128)S(1)}, f32[16,4,8]{0,2,1:T(8,128)}, u32[]{:S(2)}) copy-start(f32[16,4,8]{0,2,1:T(8,128)} %param.11) | copy-start | bytes 6148
  304.2 16.6 %copy-start.8 = (s32[16]{0:T(128)S(1)}, s32[16]{0:T(128)}, u32[]{:S(2)}) copy-start(s32[16]{0:T(128)} %param.14) | copy-start | bytes 196
  309.9 39.2 %all-to-all-start.2 = ((bf16[64,4,2,1024]{3,2,1,0:T(2,128)(2,1)}), bf16[64,4,2,1024]{3,2,1,0:T(2,128)(2,1)}, u32[]{:S(2)}, u32[]{:S(2)}) async-start(bf16[64,4,2,1024]{3,2,1,0:T(2,128)(2,1)} %bitcast.82), calls=%async_computation.2 | async-start | bytes 2097152 | tf_op jit(solution)/shard_map/all_to_all | solution.py:90
